TPU v7x, 32 devices: a whole 2x2x4 slice. The times are simulated.
32 devices in a mesh: rep: 2 (over x), seq: 4 (over y, core), head: 4 (over z).
Axes of the slice: x: 2, y: 2, z: 4, core: 2. Of those that a mesh axis runs over, the one named last changes fastest.
Arguments:
- query_rows: bfloat16 [2048, 8192], P(('rep', 'seq'), 'head'), parts along dimension 0, may hold values from -128 to 128
- span_kv: bfloat16 [2, 2048, 1024], P(None, ('rep', 'seq'), 'head'), parts along dimension 1, may hold values from -6 to 6
- cache_kv: bfloat16 [2, 4096, 1024], P(None, ('rep', 'seq'), 'head'), parts along dimension 1, may hold values from -6 to 6
- cache_len: int32 [8], P(('rep', 'seq')), parts along dimension 0, may hold values from 1 to 512, 1024 in all
Outputs:
- attended: bfloat16 [2048, 8192], P(('rep', 'seq'), 'head'), parts along dimension 0
There are 2 independent parts, one for each index of `rep`. A program takes and returns all parts, laid end to end along the dimension named above; each array names one. Nothing has to cross between parts.
Inputs may be any that keep to these rules, and one draw needn't show every extreme that they name: `cache_len`: the earlier prompt is the filled slots of the instances in order; every instance has at least one filled slot and some instance is full.
All inputs are finite; a program needn't handle non-finite values. No bound on the sum of `cache_len` on one device may be relied on, other than what follows from the above.
Results may differ from a plain program's by a relative error of at most 0.007.
Values may be sent and summed in bfloat16 or wider, within the bound.
No kernel may reach another device: no remote copies, remote signals or barrier semaphores. Data moves between devices by JAX's collectives and lax.ppermute only.
A program may use at most 64 MiB of HBM per device.

v0:
```python
import jax
import jax.numpy as jnp
from jax import lax
from jax.sharding import PartitionSpec as P

HD = 128
blocked_tag = 1073741824
neg_value = -1e30


def fold_rows(carry_state, queries, positions, block_keys, block_values, block_tags):
    row_count = block_keys.shape[0]
    block_rows = 128
    block_count = row_count // block_rows
    kv_local = block_keys.shape[1] // HD
    key_blocks = block_keys.reshape(block_count, block_rows, kv_local, HD)
    value_blocks = block_values.reshape(block_count, block_rows, kv_local, HD)
    tag_blocks = block_tags.reshape(block_count, block_rows)

    def attend(carry_in, keys_in, values_in, tags_in):
        running_max, running_sum, running_out = carry_in
        scores = jnp.einsum(
            "qkgd,rkd->kgqr", queries, keys_in, preferred_element_type=jnp.float32
        ) * HD ** (-0.5)
        visible = tags_in[None, :] <= positions[:, None]
        scores = jnp.where(visible, scores, jnp.float32(neg_value))
        new_max = jnp.maximum(running_max, jnp.max(scores, axis=-1))
        rescale = jnp.exp(running_max - new_max)
        weights = jnp.where(visible, jnp.exp(scores - new_max[..., None]), jnp.float32(0.0))
        running_sum = running_sum * rescale + jnp.sum(weights, axis=-1)
        running_out = running_out * rescale[..., None] + jnp.einsum(
            "kgqr,rkd->kgqd",
            weights.astype(jnp.bfloat16),
            values_in,
            preferred_element_type=jnp.float32,
        )
        return (new_max, running_sum, running_out)

    def advance(carry_in, block_in):
        keys_in, values_in, tags_in = block_in
        carry_out = attend(carry_in, keys_in, values_in, tags_in)
        return (carry_out, None)

    carry_state, unused = lax.scan(advance, carry_state, (key_blocks, value_blocks, tag_blocks))
    return carry_state


def body(query_rows, span_kv, cache_kv, cache_len):
    tok_rows = query_rows.shape[0]
    kv_width = span_kv.shape[2]
    kv_local = kv_width // HD
    q_group = query_rows.shape[1] // kv_width
    own_index = lax.axis_index("seq")
    positions = own_index * tok_rows + jnp.arange(tok_rows, dtype=jnp.int32)
    queries = query_rows.reshape(tok_rows, kv_local, q_group, HD)
    slot_ids = jnp.arange(cache_kv.shape[1], dtype=jnp.int32)
    cache_tags = jnp.where(slot_ids < cache_len[0], jnp.int32(-1), jnp.int32(blocked_tag))
    carry_state = (
        jnp.full((kv_local, q_group, tok_rows), neg_value, jnp.float32),
        jnp.zeros((kv_local, q_group, tok_rows), jnp.float32),
        jnp.zeros((kv_local, q_group, tok_rows, HD), jnp.float32),
    )
    joined_keys = jnp.concatenate([cache_kv[0], span_kv[0]], axis=0)
    joined_values = jnp.concatenate([cache_kv[1], span_kv[1]], axis=0)
    joined_tags = jnp.concatenate([cache_tags, positions], axis=0)
    carry_state = fold_rows(
        carry_state,
        queries,
        positions,
        lax.all_gather(joined_keys, "seq", axis=0, tiled=True),
        lax.all_gather(joined_values, "seq", axis=0, tiled=True),
        lax.all_gather(joined_tags, "seq", axis=0, tiled=True),
    )
    running_max, running_sum, running_out = carry_state
    result = running_out / running_sum[..., None]
    result = jnp.transpose(result, (2, 0, 1, 3)).reshape(tok_rows, kv_local * q_group * HD)
    return result.astype(jnp.bfloat16)


def solution(mesh):
    in_specs = (
        P(("rep", "seq"), "head"),
        P(None, ("rep", "seq"), "head"),
        P(None, ("rep", "seq"), "head"),
        P(("rep", "seq")),
    )
    out_specs = P(("rep", "seq"), "head")
    return jax.shard_map(body, mesh=mesh, in_specs=in_specs, out_specs=out_specs, check_vma=False)
```

profile of v0, /device:TPU:0, one launch (start us, length us, event | category | flops | bytes accessed | tf_op | source)
XLA Modules:
  0.0 155.0 jit_solution(731224061644751360)
XLA Ops:
  11.1 1.3 copy.17
  12.4 1.6 %copy.20 = bf16[256,2,8,128]{3,0,2,1:T(8,128)(2,1)S(1)} copy(bf16[256,2,8,128]{0,3,2,1:T(8,128)(2,1)} %bitcast.62) | data formatting | bytes 2097152
  14.0 6.2 %all-gather = s32[4,1,768]{2,1,0:T(1,128)S(1)} all-gather(s32[1,1,768]{2,1,0:T(1,128)S(1)} %reshape.22), channel_id=1, replica_groups=mesh['rep'=2,'seq'=4,'head'=4] {'seq'}, dimensions={0}, use_global_device_ids=true | all-gather | bytes 15360 | tf_op jit(solution)/shard_map/all_gather | solution.py:72
  20.2 11.8 %all-gather.6.cloned.1.call-done = bf16[3072,256]{1,0:T(8,128)(2,1)} async-done(((bf16[768,256]{1,0:T(8,128)(2,1)}), bf16[3072,256]{1,0:T(8,128)(2,1)}) %all-gather.6.cloned.1.call-update) | async-done | bytes 1572880 | tf_op jit(solution)/shard_map/all_gather | solution.py:71
  32.0 3.5 %reshape.28 = bf16[24,128,2,128]{3,2,1,0:T(2,128)(2,1)} reshape(bf16[3072,256]{1,0:T(8,128)(2,1)} %all-gather.6.cloned.1.call-done) | data formatting | bytes 3145728 | tf_op jit(solution)/shard_map/reshape | solution.py:17
  35.5 17.7 %all-gather.4.cloned.1.call-done = bf16[3072,256]{1,0:T(8,128)(2,1)} async-done(((bf16[768,256]{1,0:T(8,128)(2,1)}), bf16[3072,256]{1,0:T(8,128)(2,1)}) %all-gather.4.cloned.1.call-update) | async-done | bytes 1572880 | tf_op jit(solution)/shard_map/all_gather | solution.py:70
  53.2 3.5 %reshape.27 = bf16[24,128,2,128]{3,2,1,0:T(2,128)(2,1)} reshape(bf16[3072,256]{1,0:T(8,128)(2,1)} %all-gather.4.cloned.1.call-done) | data formatting | bytes 3145728 | tf_op jit(solution)/shard_map/reshape | solution.py:16
  56.8 88.7 %while.15 = (s32[]{:T(128)}, f32[2,8,256]{2,1,0:T(8,128)S(1)}, f32[2,8,256]{2,1,0:T(8,128)S(1)}, f32[2,8,256,128]{3,2,1,0:T(8,128)S(1)}, s32[24,128]{1,0:T(8,128...) while((s32[]{:T(128)}, f32[2,8,256]{2,1,0:T(8,128)S(1)}, ...), condition=%wide.region_3.4_spmd.clone, body=%wide.region_0.3_spmd.clone.sunk | while | flops 276877568 | bytes 12324493 | solution.py:44
  58.9 1.5 fusion.34
  62.6 1.5 fusion.34
  66.3 1.5 fusion.34
  70.0 1.5 fusion.34
  73.7 1.5 fusion.34
  77.4 1.5 fusion.34
  81.1 1.5 fusion.34
  84.8 1.5 fusion.34
  88.5 1.5 fusion.34
  92.2 1.5 fusion.34
  95.9 1.5 fusion.34
  99.5 1.5 fusion.34
  103.2 1.5 fusion.34
  106.9 1.5 fusion.34
  110.6 1.5 fusion.34
  114.3 1.5 fusion.34
  118.0 1.5 fusion.34
  121.7 1.5 fusion.34
  125.4 1.5 fusion.34
  129.1 1.5 fusion.34
  132.8 1.5 fusion.34
  136.5 1.5 fusion.34
  140.2 1.5 fusion.34
  143.9 1.5 fusion.34
  (236 shorter events, 56.7 us)
Async XLA Ops:
  6.5 4.6 %copy-start = (bf16[256,2048]{1,0:T(8,128)(2,1)S(1)}, bf16[256,2048]{1,0:T(8,128)(2,1)}, u32[]{:S(2)}) copy-start(bf16[256,2048]{1,0:T(8,128)(2,1)} %param.6) | copy-start | bytes 3145732
  6.5 25.5 %all-gather.6.cloned.1.call-start = ((), (), s32[]{:S(2)}) async-start(), calls=%async_computation.1 | async-start | bytes 1966080 | tf_op jit(solution)/shard_map/all_gather | solution.py:71
  9.5 43.8 %all-gather.4.cloned.1.call-start = ((), (), s32[]{:S(2)}) async-start(), calls=%async_computation | async-start | bytes 1966080 | tf_op jit(solution)/shard_map/all_gather | solution.py:70
Sparse Core Ops, SparseCore 0:
  9.6 22.3 all-gather.5
  33.6 19.6 all-gather.3
where the time goes:
time: 156 us; the launch traced here: 155 us
  matrix products  47.6 us (31%)
  local copies, waits for them, and re-layouts  37.6 us (24%)
  waiting for transfers between devices  29.5 us (19%)
  other arithmetic  17.7 us (11%)
  between operations  14.2 us (9%)
  blocking collectives  6.19 us (4%)
  loops' own time  2.08 us (1%)
    dot_general x24, matrix products, attend(): jnp.einsum('kgqr,rkd->kgqd', weights.astype(jnp.bfloat16), values_in, pre...  36.4 us
    dynamic_slice x24, local copies, waits for them, and re-layouts, fold_rows(): lax.scan(advance, carry_state, (key_blocks, value_blocks, tag_blocks))  23.3 us
    all_gather x1, waiting for transfers between devices, body(): lax.all_gather(joined_keys, 'seq', axis=0, tiled=True)  17.7 us
    reduce_sum x24, other arithmetic, attend(): running_sum = running_sum * rescale + jnp.sum(weights, axis=-1)  12.7 us
    all_gather x1, waiting for transfers between devices, body(): lax.all_gather(joined_values, 'seq', axis=0, tiled=True)  11.8 us
    dot_general x24, matrix products, attend(): jnp.einsum('qkgd,rkd->kgqr', queries, keys_in, preferred_element_type=jnp...  11.2 us
    all_gather x1, blocking collectives, body(): lax.all_gather(joined_tags, 'seq', axis=0, tiled=True)  6.19 us
    unnamed x6, local copies, waits for them, and re-layouts  4.17 us
  transfers between devices with their start and end apart: 2, of which 2 were waited for; matrix products, arithmetic and copies ran while one was open for 5% of the time, Pallas kernels for 0%

commit v1 on v0

--- a/solution.py
+++ b/solution.py
@@ -6,6 +6,27 @@
 HD = 128
 blocked_tag = 1073741824
 neg_value = -1e30
+
+
+def gather_around(shard, axis, dim):
+    length, index, span = (lax.axis_size(axis), lax.axis_index(axis), shard.shape[dim])
+    right = [(i, (i + 1) % length) for i in range(length)]
+    left = [(i, (i - 1) % length) for i in range(length)]
+    out = jnp.zeros((*shard.shape[:dim], length * span, *shard.shape[dim + 1 :]), shard.dtype)
+    out = lax.dynamic_update_slice_in_dim(out, shard, index * span, axis=dim)
+    from_left = from_right = shard
+    halfway = length // 2
+    for lap in range(1, halfway + 1):
+        from_left = lax.ppermute(from_left, axis, right)
+        out = lax.dynamic_update_slice_in_dim(
+            out, from_left, (index - lap) % length * span, axis=dim
+        )
+        if lap < length - halfway:
+            from_right = lax.ppermute(from_right, axis, left)
+            out = lax.dynamic_update_slice_in_dim(
+                out, from_right, (index + lap) % length * span, axis=dim
+            )
+    return out
 
 
 def fold_rows(carry_state, queries, positions, block_keys, block_values, block_tags):
@@ -67,7 +88,7 @@
         carry_state,
         queries,
         positions,
-        lax.all_gather(joined_keys, "seq", axis=0, tiled=True),
+        gather_around(joined_keys, "seq", 0),
         lax.all_gather(joined_values, "seq", axis=0, tiled=True),
         lax.all_gather(joined_tags, "seq", axis=0, tiled=True),
     )

time: 156 us -> 192 us (1.23); the launches traced: 155 us -> 189 us
  local copies, waits for them, and re-layouts: 37.6 us -> 67.3 us
  waiting for transfers between devices: 29.5 us -> 6.41 us
  matrix products: 47.6 us -> 67.9 us
  starting transfers between devices: 0.04 us -> 6.3 us
    dot_general x24, matrix products: 11.2 us -> 31.5 us  [attend(): jnp.einsum('qkgd,rkd->kgqr', queries, keys_in, preferred_element_type=jnp...]
    all_gather x1 -> x0, waiting for transfers between devices: 17.7 us -> none  [body(): lax.all_gather(joined_keys, 'seq', axis=0, tiled=True)]
    le x24, local copies, waits for them, and re-layouts: 0.22 us -> 16.5 us  [attend(): visible = tags_in[None, :] <= positions[:, None]]
    all_gather x1, waiting for transfers between devices: 11.8 us -> 0.01 us  [body(): lax.all_gather(joined_values, 'seq', axis=0, tiled=True)]
    unnamed x6 -> x10, local copies, waits for them, and re-layouts: 4.17 us -> 11.2 us
    ppermute x0 -> x3, waiting for transfers between devices: none -> 6.39 us  [the longest x2 6.39 us: gather_around(): from_left = lax.ppermute(from_left, axis, right)]
    ppermute x0 -> x3, starting transfers between devices: none -> 6.29 us  [the longest x2 4.27 us: gather_around(): from_left = lax.ppermute(from_left, axis, right)]
    dynamic_update_slice x0 -> x4, local copies, waits for them, and re-layouts: none -> 5.24 us  [the longest x2 2.61 us: gather_around(): lax.dynamic_update_slice_in_dim(out, from_left, (index - lap) % length *...]
  transfers between devices with their start and end apart: 2 -> 4, of which waited for: 2 -> 1; matrix products, arithmetic and copies ran while one was open for 5% -> 12% of each run, Pallas kernels for 0% -> 0%
where the time goes in v1:
time: 192 us; the launch traced here: 189 us
  matrix products  67.9 us (35%)
  local copies, waits for them, and re-layouts  67.3 us (35%)
  other arithmetic  17.5 us (9%)
  between operations  14.1 us (7%)
  blocking collectives  7.5 us (4%)
  waiting for transfers between devices  6.41 us (3%)
  starting transfers between devices  6.3 us (3%)
    dot_general x24, matrix products, attend(): jnp.einsum('kgqr,rkd->kgqd', weights.astype(jnp.bfloat16), values_in, pre...  36.4 us
    dot_general x24, matrix products, attend(): jnp.einsum('qkgd,rkd->kgqr', queries, keys_in, preferred_element_type=jnp...  31.5 us
    dynamic_slice x24, local copies, waits for them, and re-layouts, fold_rows(): lax.scan(advance, carry_state, (key_blocks, value_blocks, tag_blocks))  21.4 us
    le x24, local copies, waits for them, and re-layouts, attend(): visible = tags_in[None, :] <= positions[:, None]  16.5 us
    reduce_sum x24, other arithmetic, attend(): running_sum = running_sum * rescale + jnp.sum(weights, axis=-1)  12.7 us
    unnamed x10, local copies, waits for them, and re-layouts  11.2 us
    all_gather x1, blocking collectives, body(): lax.all_gather(joined_tags, 'seq', axis=0, tiled=True)  7.5 us
    ppermute x2, waiting for transfers between devices, gather_around(): from_left = lax.ppermute(from_left, axis, right)  6.39 us
  transfers between devices with their start and end apart: 4, of which 1 were waited for; matrix products, arithmetic and copies ran while one was open for 12% of the time, Pallas kernels for 0%

profile of v1, /device:TPU:0, one launch (start us, length us, event | category | flops | bytes accessed | tf_op | source)
XLA Modules:
  0.0 188.8 jit_solution(8410685243780598814)
XLA Ops:
  10.1 2.0 %collective-permute-start.1 = (bf16[768,256]{1,0:T(8,128)(2,1)S(1)}, bf16[768,256]{1,0:T(8,128)(2,1)}, u32[]{:S(2)}, u32[]{:S(2)}) collective-permute-start(bf16[768,256]{1,0:T(8,128)(2,1)S(1)} %pad_maximum_fusion), channel_id=1, source_target_pairs={{0,12},{4,0},{8,4},{12,8},{1,13},{5,1},{9,5},{13,9},{2,14},{6,2},{... | collective-permute-start | bytes 1179656 | tf_op jit(solution)/shard_map/ppermute | solution.py:25
  12.8 6.4 %collective-permute-done = bf16[768,256]{1,0:T(8,128)(2,1)} collective-permute-done((bf16[768,256]{1,0:T(8,128)(2,1)S(1)}, bf16[768,256]{1,0:T(8,128)(2,1)}, u32[]{:S(2)}, u32[]{:S(2)}) %collective-permute-start) | collective-permute-done | bytes 393248 | tf_op jit(solution)/shard_map/ppermute | solution.py:20
  19.1 3.8 %collective-permute-start.2 = (bf16[768,256]{1,0:T(8,128)(2,1)}, bf16[768,256]{1,0:T(8,128)(2,1)}, u32[]{:S(2)}, u32[]{:S(2)}) collective-permute-start(bf16[768,256]{1,0:T(8,128)(2,1)} %collective-permute-done), channel_id=1, source_target_pairs={{0,4},{4,8},{8,12},{12,0},{1,5},{5,9},{9,13},{13,1},{2,6},{6,10},{... | collective-permute-start | bytes 1179656 | tf_op jit(solution)/shard_map/ppermute | solution.py:20
  27.0 1.6 copy.26
  28.7 7.5 %all-gather = s32[4,1,768]{2,1,0:T(1,128)} all-gather(s32[1,1,768]{2,1,0:T(1,128)} %reshape.22), channel_id=1, replica_groups=mesh['rep'=2,'seq'=4,'head'=4] {'seq'}, dimensions={0}, use_global_device_ids=true | all-gather | bytes 15360 | tf_op jit(solution)/shard_map/all_gather | solution.py:93
  37.5 1.8 constant_dynamic-update-slice_fusion.3
  39.3 1.9 %copy.20 = bf16[768,256]{0,1:T(8,128)(2,1)} copy(bf16[768,256]{1,0:T(8,128)(2,1)} %collective-permute-done) | data formatting | bytes 786432 | tf_op jit(solution)/shard_map/ppermute | solution.py:20
  42.4 1.8 constant_dynamic-update-slice_fusion.2
  47.0 2.9 %copy.35 = bf16[32,8,24,128]{3,2,1,0:T(8,128)(2,1)} copy(bf16[32,8,24,128]{3,1,2,0:T(8,128)(2,1)} %bitcast.19) | data formatting | bytes 3145728
  49.9 2.9 %copy.25 = bf16[24,128,2,128]{3,1,2,0:T(8,128)(2,1)} copy(bf16[24,128,2,128]{1,0,3,2:T(8,128)(2,1)} %bitcast.66) | data formatting | bytes 3145728
  52.8 3.5 %reshape.27 = bf16[24,128,2,128]{3,2,1,0:T(2,128)(2,1)} reshape(bf16[3072,256]{1,0:T(8,128)(2,1)} %all-gather.3.cloned.1.call-done) | data formatting | bytes 3145728 | tf_op jit(solution)/shard_map/reshape | solution.py:38
  56.3 123.0 %while.15 = (s32[]{:T(128)}, f32[2,8,256]{2,1,0:T(8,128)S(1)}, f32[2,8,256]{2,1,0:T(8,128)S(1)}, f32[2,8,256,128]{3,2,1,0:T(8,128)S(1)}, s32[24,128]{1,0:T(8,128...) while((s32[]{:T(128)}, f32[2,8,256]{2,1,0:T(8,128)S(1)}, ...), condition=%wide.region_3.4_spmd.clone, body=%wide.region_0.3_spmd.clone.sunk | while | flops 276877568 | bytes 12193425 | solution.py:65
  59.8 1.5 fusion.37
  65.0 1.5 fusion.37
  70.1 1.5 fusion.37
  75.2 1.5 fusion.37
  80.4 1.5 fusion.37
  85.5 1.5 fusion.37
  90.6 1.5 fusion.37
  95.7 1.5 fusion.37
  100.9 1.5 fusion.37
  106.0 1.5 fusion.37
  111.1 1.5 fusion.37
  116.3 1.5 fusion.37
  121.4 1.5 fusion.37
  126.5 1.5 fusion.37
  131.6 1.5 fusion.37
  136.8 1.5 fusion.37
  141.9 1.5 fusion.37
  147.0 1.5 fusion.37
  162.4 1.5 fusion.37
  177.7 1.5 fusion.37
  (251 shorter events, 106.5 us)
Async XLA Ops:
  6.5 46.2 %all-gather.3.cloned.1.call-start = ((), (), s32[]{:S(2)}) async-start(), calls=%async_computation | async-start | bytes 1966080 | tf_op jit(solution)/shard_map/all_gather | solution.py:92
  7.5 18.2 %copy-start = (bf16[256,2048]{1,0:T(8,128)(2,1)S(1)}, bf16[256,2048]{1,0:T(8,128)(2,1)}, u32[]{:S(2)}) copy-start(bf16[256,2048]{1,0:T(8,128)(2,1)} %param.6) | copy-start | bytes 3145732
  9.6 9.6 %collective-permute-start = (bf16[768,256]{1,0:T(8,128)(2,1)S(1)}, bf16[768,256]{1,0:T(8,128)(2,1)}, u32[]{:S(2)}, u32[]{:S(2)}) collective-permute-start(bf16[768,256]{1,0:T(8,128)(2,1)S(1)} %pad_maximum_fusion), channel_id=1, source_target_pairs={{0,4},{4,8},{8,12},{12,0},{1,5},{5,9},{9,13},{13,1},{2,6},{6,10},{... | collective-permute-start | bytes 1179656 | tf_op jit(solution)/shard_map/ppermute | solution.py:20
  10.1 31.1 %collective-permute-start.1 = (bf16[768,256]{1,0:T(8,128)(2,1)S(1)}, bf16[768,256]{1,0:T(8,128)(2,1)}, u32[]{:S(2)}, u32[]{:S(2)}) collective-permute-start(bf16[768,256]{1,0:T(8,128)(2,1)S(1)} %pad_maximum_fusion), channel_id=1, source_target_pairs={{0,12},{4,0},{8,4},{12,8},{1,13},{5,1},{9,5},{13,9},{2,14},{6,2},{... | collective-permute-start | bytes 1179656 | tf_op jit(solution)/shard_map/ppermute | solution.py:25
  19.1 25.9 %collective-permute-start.2 = (bf16[768,256]{1,0:T(8,128)(2,1)}, bf16[768,256]{1,0:T(8,128)(2,1)}, u32[]{:S(2)}, u32[]{:S(2)}) collective-permute-start(bf16[768,256]{1,0:T(8,128)(2,1)} %collective-permute-done), channel_id=1, source_target_pairs={{0,4},{4,8},{8,12},{12,0},{1,5},{5,9},{9,13},{13,1},{2,6},{6,10},{... | collective-permute-start | bytes 1179656 | tf_op jit(solution)/shard_map/ppermute | solution.py:20
  52.7 3.5 %copy-start.1 = (f32[2,8,256]{2,1,0:T(8,128)S(1)}, f32[2,8,256]{2,1,0:T(8,128)}, u32[]{:S(2)}) copy-start(f32[2,8,256]{2,1,0:T(8,128)} %custom-call.1) | copy-start | bytes 49156
Sparse Core Ops, SparseCore 0:
  9.6 26.5 all-gather.2
